TPU v7x, 32 devices: a whole 2x2x4 slice. The times are simulated.
32 devices in a mesh: row: 4 (over z), col: 4 (over y, core), pix: 2 (over x).
Axes of the slice: x: 2, y: 2, z: 4, core: 2. Of those that a mesh axis runs over, the one named last changes fastest.
Arguments:
- sample_frames: bfloat16 [4096, 16384], P(('row', 'col'), 'pix'), may hold values from 0.14 to 26
- reference_frames: bfloat16 [4096, 16384], P(('row', 'col'), 'pix'), may hold values from 0.14 to 26
- gain: float32 [16384], P('pix'), may hold values from 0.5 to 2
- flat: float32 [16384], P('pix'), may hold values from 0.6 to 1.6
- qbin: int32 [16384], P('pix'), may hold values from 0 to 31
- region: int32 [16384], P('pix'), may hold values 0 or 1
- live: int32 [16384], P('pix'), may hold values 0 or 1
Outputs:
- twotime: float32 [4096, 4, 4, 256], P('row', None, 'col', 'pix')
All inputs are finite; a program needn't handle non-finite values. No bound on the sum of `region` or of `live` on one device may be relied on, other than what follows from the above.
Results may differ from a plain program's by a relative error of at most 0.0039.
Values may be sent and summed in bfloat16 or wider, within the bound.
No kernel may reach another device: no remote copies, remote signals or barrier semaphores. Data moves between devices by JAX's collectives and lax.ppermute only.
A program may use at most 128 MiB of HBM per device.

v0:
```python
import math

import jax
import jax.numpy as jnp
from jax import lax
from jax.sharding import PartitionSpec as P

QBINS = 32


def on_device(sample_frames, reference_frames, gain, flat, qbin, region, live):
    block = sample_frames.shape[0]
    factor = gain / flat
    select = (qbin[None, :] == jnp.arange(QBINS, dtype=jnp.int32)[:, None]).astype(jnp.float32)
    ref_select = select * (live * (1 - region)).astype(jnp.float32)[None, :]
    sample_weight = (live * region).astype(jnp.float32)
    corrected_sample = sample_frames.astype(jnp.float32) * factor
    corrected_reference = reference_frames.astype(jnp.float32) * factor
    sums_sample = jnp.dot(corrected_sample, ref_select.T, precision=lax.Precision.HIGHEST)
    sums_reference = jnp.dot(corrected_reference, ref_select.T, precision=lax.Precision.HIGHEST)
    counts = jnp.sum(ref_select, axis=1)
    sums_sample, sums_reference, counts = lax.psum((sums_sample, sums_reference, counts), "pix")
    mean_sample = (sums_sample + 1.0) / (counts + 1.0)
    mean_reference = (sums_reference + 1.0) / (counts + 1.0)
    spread_sample = jnp.dot(mean_sample, select, precision=lax.Precision.HIGHEST)
    spread_reference = jnp.dot(mean_reference, select, precision=lax.Precision.HIGHEST)
    delta_sample = ((corrected_sample / spread_sample - 1.0) * sample_weight).astype(jnp.bfloat16)
    delta_reference = (corrected_reference / spread_reference - 1.0).astype(jnp.bfloat16)
    sample_rows = lax.all_gather(delta_sample, "col", axis=0, tiled=True)
    partial_value = lax.dot_general(
        sample_rows,
        lax.all_gather(delta_reference, "row", axis=0, tiled=True),
        (((1,), (1,)), ((), ())),
        preferred_element_type=jnp.float32,
    )
    groups = lax.axis_size("row")
    scale = 1.0 / math.sqrt(gain.shape[0] * lax.axis_size("pix"))
    partial_value = (partial_value * scale).reshape(sample_rows.shape[0], groups, block)
    whole = lax.psum(partial_value, "pix")
    width = block // lax.axis_size("pix")
    mine = lax.dynamic_slice_in_dim(whole, lax.axis_index("pix") * width, width, 2)
    return mine[:, :, None, :]


def solution(mesh):
    return jax.shard_map(
        on_device,
        mesh=mesh,
        in_specs=(
            P(("row", "col"), "pix"),
            P(("row", "col"), "pix"),
            P("pix"),
            P("pix"),
            P("pix"),
            P("pix"),
            P("pix"),
        ),
        out_specs=P("row", None, "col", "pix"),
        check_vma=False,
    )
```

profile of v0, /device:TPU:16, one launch (start us, length us, event | category | flops | bytes accessed | tf_op | source)
XLA Modules:
  0.0 596.8 jit_solution(18286605986021742596)
XLA Ops:
  6.5 0.0 copy-start
  6.5 0.0 all-reduce.6.cloned.1.call-start
  6.5 0.8 multiply_convert_fusion.1
  7.3 0.8 div.23
  8.1 1.5 select_reduce_fusion
  9.6 9.2 %fusion.5 = f32[256,32]{1,0:T(8,128)} fusion(bf16[256,8192]{1,0:T(8,128)(2,1)} %param.8, f32[8192]{0:T(1024)S(1)} %div.23, f32[8192]{0:T(1024)S(1)} %get-tuple-element.8, s32[8192]{0:T(1024)} %param.11), kind=kOutput, calls=%fused_computation.8 | convolution fusion | flops 810024960 | bytes 4325376 | tf_op jit(solution)/shard_map/dot_general | solution.py:20
  18.8 9.2 %fusion.6 = f32[256,32]{1,0:T(8,128)} fusion(bf16[256,8192]{1,0:T(8,128)(2,1)} %param.7, f32[8192]{0:T(1024)S(1)} %div.23, f32[8192]{0:T(1024)S(1)} %get-tuple-element.8, s32[8192]{0:T(1024)} %param.11), kind=kOutput, calls=%fused_computation.10 | convolution fusion | flops 810024960 | bytes 4325376 | tf_op jit(solution)/shard_map/dot_general | solution.py:19
  28.0 0.0 all-reduce.6.cloned.1.call-update
  28.1 0.0 all-gather.3.cloned.1.call-start
  28.1 24.7 %all-reduce.6.cloned.1.call-done = (f32[256,32]{1,0:T(8,128)}, f32[32]{0:T(128)}, f32[256,32]{1,0:T(8,128)}) async-done(((f32[256,32]{1,0:T(8,128)}, f32[32]{0:T(128)}, f32[256,32]{1,0:T(8,128)}), (f32[256,32]{1,0:T(8,128)}, f32[32]{0:T(128)}, f32[256,32]{1,0:T(8,128)})) %all-reduce.6.cloned.1.call-update) | async-done | bytes 65680 | tf_op jit(solution)/shard_map/psum | solution.py:22
  52.9 0.6 broadcast_add_fusion
  53.5 0.0 copy-done
  53.5 0.0 copy-start.1
  53.5 7.9 %fusion.4 = bf16[256,8192]{1,0:T(8,128)(2,1)} fusion(bf16[256,8192]{1,0:T(8,128)(2,1)} %param.7, f32[8192]{0:T(1024)S(1)} %get-tuple-element.9, f32[8192]{0:T(1024)S(1)} %div.23, s32[8192]{0:T(1024)S(1)} %copy-done, f32[256,32]{1,0:T(8,128)} %get-tuple-element.5, f32[32]{0:T(128)S(1)} %broadcast_add_fusion), kind=kOutput, calls=%fused_computation.6 | convolution fusion | flops 818167808 | bytes 8519808 | tf_op jit(solution)/shard_map/dot_general | solution.py:25
  61.4 0.0 all-gather.3.cloned.1.call-update
  61.4 0.2 all-gather.5.cloned.1.call-start
  61.6 0.0 copy-done.1
  61.7 7.6 %fusion.1 = bf16[256,8192]{1,0:T(8,128)(2,1)} fusion(bf16[256,8192]{1,0:T(8,128)(2,1)} %param.8, f32[8192]{0:T(1024)S(1)} %div.23, s32[8192]{0:T(1024)S(1)} %copy-done, f32[256,32]{1,0:T(8,128)S(1)} %copy-done.1, f32[32]{0:T(128)S(1)} %broadcast_add_fusion), kind=kOutput, calls=%fused_computation.2 | convolution fusion | flops 816070656 | bytes 8487040 | tf_op jit(solution)/shard_map/dot_general | solution.py:26
  69.2 0.0 all-gather.5.cloned.1.call-update
  69.3 0.0 all-reduce.4.cloned.1.call-start
  69.3 98.4 %all-gather.3.cloned.1.call-done = bf16[1024,8192]{1,0:T(8,128)(2,1)} async-done(((bf16[256,8192]{1,0:T(8,128)(2,1)}), bf16[1024,8192]{1,0:T(8,128)(2,1)}) %all-gather.3.cloned.1.call-update) | async-done | bytes 16777232 | tf_op jit(solution)/shard_map/all_gather | solution.py:29
  167.7 286.7 %all-gather.5.cloned.1.call-done = bf16[1024,8192]{1,0:T(8,128)(2,1)} async-done(((bf16[256,8192]{1,0:T(8,128)(2,1)}), bf16[1024,8192]{1,0:T(8,128)(2,1)}) %all-gather.5.cloned.1.call-update) | async-done | bytes 16777232 | tf_op jit(solution)/shard_map/all_gather | solution.py:32
  454.4 24.3 %convolution_multiply_fusion = f32[1024,1024]{0,1:T(8,128)} fusion(bf16[1024,8192]{1,0:T(8,128)(2,1)} %all-gather.3.cloned.1.call-done, bf16[1024,8192]{1,0:T(8,128)(2,1)} %all-gather.5.cloned.1.call-done), kind=kOutput, calls=%fused_computation.13 | convolution fusion | flops 17180917760 | bytes 37748736 | tf_op jit(solution)/shard_map/dot_general | solution.py:30
  478.7 0.0 all-reduce.4.cloned.1.call-update
  478.8 108.0 %all-reduce.4.cloned.1.call-done = f32[1024,4,256]{0,2,1:T(8,128)} async-done(((f32[1024,4,256]{0,2,1:T(8,128)}), f32[1024,4,256]{0,2,1:T(8,128)}) %all-reduce.4.cloned.1.call-update) | async-done | bytes 4194320 | tf_op jit(solution)/shard_map/psum | solution.py:39
  586.7 1.7 constant_dynamic-slice_fusion
  588.4 1.8 copy.9
Async XLA Ops:
  6.5 47.0 %copy-start = (s32[8192]{0:T(1024)S(1)}, s32[8192]{0:T(1024)}, u32[]{:S(2)}) copy-start(s32[8192]{0:T(1024)} %param.11) | copy-start | bytes 98308
  6.5 46.3 %all-reduce.6.cloned.1.call-start = ((), (), s32[]{:S(2)}) async-start(), calls=%async_computation.3 | async-start | bytes 525312 | tf_op jit(solution)/shard_map/psum | solution.py:22
  28.1 139.6 %all-gather.3.cloned.1.call-start = ((), (), s32[]{:S(2)}) async-start(), calls=%async_computation | async-start | bytes 20971520 | tf_op jit(solution)/shard_map/all_gather | solution.py:29
  53.5 8.2 %copy-start.1 = (f32[256,32]{1,0:T(8,128)S(1)}, f32[256,32]{1,0:T(8,128)}, u32[]{:S(2)}) copy-start(f32[256,32]{1,0:T(8,128)} %get-tuple-element.7) | copy-start | bytes 98308
  61.4 393.0 %all-gather.5.cloned.1.call-start = ((), (), s32[]{:S(2)}) async-start(), calls=%async_computation.1 | async-start | bytes 20971520 | tf_op jit(solution)/shard_map/all_gather | solution.py:32
  69.3 517.4 %all-reduce.4.cloned.1.call-start = ((), (), s32[]{:S(2)}) async-start(), calls=%async_computation.2 | async-start | bytes 8388608 | tf_op jit(solution)/shard_map/psum | solution.py:39
Sparse Core Ops, SparseCore 0:
  28.2 24.6 all-reduce.5
  61.5 106.1 all-gather.2
  169.4 285.0 all-gather.4
  478.9 107.8 all-reduce.3
where the time goes:
time: 599 us; the launch traced here: 597 us
  waiting for transfers between devices  518 us (86%)
  matrix products  58.3 us (10%)
  between operations  13.2 us (2%)
    all_gather x1, waiting for transfers between devices, on_device(): lax.all_gather(delta_reference, 'row', axis=0, tiled=True)  287 us
    psum x1, waiting for transfers between devices, on_device(): whole = lax.psum(partial_value, 'pix')  108 us
    all_gather x1, waiting for transfers between devices, on_device(): sample_rows = lax.all_gather(delta_sample, 'col', axis=0, tiled=True)  98.4 us
    psum x1, waiting for transfers between devices, on_device(): lax.psum((sums_sample, sums_reference, counts), 'pix')  24.7 us
    dot_general x1, matrix products, on_device(): lax.dot_general(sample_rows, lax.all_gather(delta_reference, 'row', axis=...  24.3 us
  transfers between devices with their start and end apart: 4, of which 4 were waited for; matrix products, arithmetic and copies ran while one was open for 1% of the time, Pallas kernels for 0%

commit v1 on v0

v1 whole, which is shorter than its diff:
```python
import math

import jax
import jax.numpy as jnp
from jax import lax
from jax.sharding import PartitionSpec as P

QBINS = 32


def _swap(x, axis):
    return lax.ppermute(x, axis, [(0, 1), (1, 0)])


def on_device(sample_frames, reference_frames, gain, flat, qbin, region, live):
    block = sample_frames.shape[0]
    n_row = lax.axis_size("row")
    n_pix = lax.axis_size("pix")
    r = lax.axis_index("row")
    p = lax.axis_index("pix")
    factor = gain / flat
    select = (qbin[None, :] == jnp.arange(QBINS, dtype=jnp.int32)[:, None]).astype(jnp.float32)
    ref_select = select * (live * (1 - region)).astype(jnp.float32)[None, :]
    sample_weight = (live * region).astype(jnp.float32)
    corrected_sample = sample_frames.astype(jnp.float32) * factor
    corrected_reference = reference_frames.astype(jnp.float32) * factor
    sums_sample = jnp.dot(corrected_sample, ref_select.T, precision=lax.Precision.HIGHEST)
    sums_reference = jnp.dot(corrected_reference, ref_select.T, precision=lax.Precision.HIGHEST)
    counts = jnp.sum(ref_select, axis=1)
    stats = (sums_sample, sums_reference, counts)
    if n_pix == 2:
        other = _swap(stats, "pix")
        stats = jax.tree.map(jnp.add, stats, other)
    else:
        stats = lax.psum(stats, "pix")
    sums_sample, sums_reference, counts = stats
    mean_sample = (sums_sample + 1.0) / (counts + 1.0)
    mean_reference = (sums_reference + 1.0) / (counts + 1.0)
    spread_sample = jnp.dot(mean_sample, select, precision=lax.Precision.HIGHEST)
    spread_reference = jnp.dot(mean_reference, select, precision=lax.Precision.HIGHEST)
    delta_sample = ((corrected_sample / spread_sample - 1.0) * sample_weight).astype(jnp.bfloat16)
    delta_reference = (corrected_reference / spread_reference - 1.0).astype(jnp.bfloat16)

    arrivals = [delta_reference]
    for k in range(1, n_row):
        perm = [(i, (i + k) % n_row) for i in range(n_row)]
        arrivals.append(lax.ppermute(delta_reference, "row", perm))

    sample_rows = lax.all_gather(delta_sample, "col", axis=0, tiled=True)
    scale = 1.0 / math.sqrt(gain.shape[0] * n_pix)
    width = block // n_pix
    out = jnp.zeros((sample_rows.shape[0], n_row, width), jnp.float32)
    for k in range(n_row):
        part = lax.dot_general(
            sample_rows,
            arrivals[k],
            (((1,), (1,)), ((), ())),
            preferred_element_type=jnp.float32,
        )
        part = part * scale
        if n_pix == 2:
            keep = lax.dynamic_slice_in_dim(part, p * width, width, 1)
            give = lax.dynamic_slice_in_dim(part, (1 - p) * width, width, 1)
            mine = keep + _swap(give, "pix")
        else:
            mine = lax.psum_scatter(part, "pix", scatter_dimension=1, tiled=True)
        a = (r - k) % n_row
        out = lax.dynamic_update_slice(out, mine[:, None, :], (0, a, 0))
    return out[:, :, None, :]


def solution(mesh):
    return jax.shard_map(
        on_device,
        mesh=mesh,
        in_specs=(
            P(("row", "col"), "pix"),
            P(("row", "col"), "pix"),
            P("pix"),
            P("pix"),
            P("pix"),
            P("pix"),
            P("pix"),
        ),
        out_specs=P("row", None, "col", "pix"),
        check_vma=False,
    )
```

time: 599 us -> 462 us (0.77)
  waiting for transfers between devices: 518 us -> 366 us
  starting transfers between devices: 0.31 us -> 9.17 us
  matrix products: 58.3 us -> 66.9 us
    ppermute x0 -> x10, waiting for transfers between devices: none -> 366 us  [the longest x3 347 us: on_device(): arrivals.append(lax.ppermute(delta_reference, 'row', perm))]
    all_gather x1 -> x0, waiting for transfers between devices: 287 us -> none  [on_device(): lax.all_gather(delta_reference, 'row', axis=0, tiled=True)]
    psum x2 -> x0, waiting for transfers between devices: 133 us -> none  [the longest x1 108 us: on_device(): whole = lax.psum(partial_value, 'pix')]
    all_gather x1, waiting for transfers between devices: 98.4 us -> 0.01 us  [on_device(): sample_rows = lax.all_gather(delta_sample, 'col', axis=0, tiled=True)]
    dot_general x1 -> x4, matrix products: 24.3 us -> 35.6 us  [on_device(): lax.dot_general(sample_rows, arrivals[k], (((1,), (1,)), ((), ())), prefe...]
    ppermute x0 -> x10, starting transfers between devices: none -> 9.17 us  [the longest x7 6.12 us: _swap(): return lax.ppermute(x, axis, [(0, 1), (1, 0)])]
  transfers between devices with their start and end apart: 4 -> 11, of which waited for: 4 -> 6; matrix products, arithmetic and copies ran while one was open for 1% -> 14% of each run, Pallas kernels for 0% -> 0%
where the time goes in v1:
time: 462 us
  waiting for transfers between devices  366 us (79%)
  matrix products  66.9 us (14%)
  between operations  13.6 us (3%)
  starting transfers between devices  9.17 us (2%)
    ppermute x3, waiting for transfers between devices, on_device(): arrivals.append(lax.ppermute(delta_reference, 'row', perm))  347 us
    dot_general x4, matrix products, on_device(): lax.dot_general(sample_rows, arrivals[k], (((1,), (1,)), ((), ())), prefe...  35.6 us
    ppermute x7, waiting for transfers between devices, _swap(): return lax.ppermute(x, axis, [(0, 1), (1, 0)])  18.8 us
  transfers between devices with their start and end apart: 11, of which 6 were waited for; matrix products, arithmetic and copies ran while one was open for 14% of the time, Pallas kernels for 0%

profile of v1, /device:TPU:16, one launch (start us, length us, event | category | flops | bytes accessed | tf_op | source)
XLA Modules:
  0.0 462.1 jit_solution(10519734714457406331)
XLA Ops:
  6.5 0.0 copy-start.1
  6.5 0.0 all-gather.2.cloned.1.call-start
  6.5 0.0 copy-start.3
  6.5 0.9 multiply_convert_fusion.1
  7.5 1.3 select_reduce_fusion
  8.8 1.6 collective-permute-start.1
  10.4 0.8 div.23
  11.2 9.0 %fusion.6 = f32[256,32]{0,1:T(8,128)S(1)} fusion(bf16[256,8192]{1,0:T(8,128)(2,1)} %param.7, f32[8192]{0:T(1024)S(1)} %div.23, f32[8192]{0:T(1024)S(1)} %get-tuple-element.5, s32[8192]{0:T(1024)} %param.11), kind=kOutput, calls=%fused_computation.10 | convolution fusion | flops 810024960 | bytes 4325376 | tf_op jit(solution)/shard_map/dot_general | solution.py:27
  20.2 0.6 collective-permute-start
  20.8 0.0 collective-permute-done.1
  20.8 3.4 collective-permute-done
  24.1 0.0 copy-done.1
  24.1 0.0 copy-done.3
  24.2 6.7 %fusion.4 = bf16[256,8192]{1,0:T(8,128)(2,1)} fusion(bf16[256,8192]{1,0:T(8,128)(2,1)S(1)} %copy-done.3, f32[8192]{0:T(1024)S(1)} %get-tuple-element.6, f32[8192]{0:T(1024)S(1)} %div.23, s32[8192]{0:T(1024)S(1)} %copy-done.1, f32[256,32]{0,1:T(8,128)S(1)} %fusion.6, f32[256,32]{0,1:T(8,128)S(1)} %collective-permute-done, f32[32]{0:T(128)S(1)} %add_add_fusion), kind=kOutput, calls=%fused_computation.6 | convolution fusion | flops 818176000 | bytes 8552576 | tf_op jit(solution)/shard_map/dot_general | solution.py:39
  30.9 0.0 all-gather.2.cloned.1.call-update
  30.9 0.0 copy-start.4
  30.9 9.1 %fusion.5 = f32[256,32]{0,1:T(8,128)S(1)} fusion(bf16[256,8192]{1,0:T(8,128)(2,1)} %param.8, f32[8192]{0:T(1024)S(1)} %div.23, f32[8192]{0:T(1024)S(1)} %get-tuple-element.5, s32[8192]{0:T(1024)S(1)} %copy-done.1), kind=kOutput, calls=%fused_computation.8 | convolution fusion | flops 810024960 | bytes 4325376 | tf_op jit(solution)/shard_map/dot_general | solution.py:28
  40.1 0.6 collective-permute-start.2
  40.7 3.4 collective-permute-done.2
  44.0 0.0 copy-done.4
  44.0 6.4 %fusion.1 = bf16[256,8192]{1,0:T(8,128)(2,1)} fusion(bf16[256,8192]{1,0:T(8,128)(2,1)S(1)} %copy-done.4, f32[8192]{0:T(1024)S(1)} %div.23, s32[8192]{0:T(1024)S(1)} %copy-done.1, f32[256,32]{0,1:T(8,128)S(1)} %fusion.5, f32[256,32]{0,1:T(8,128)S(1)} %collective-permute-done.2, f32[32]{0:T(128)S(1)} %add_add_fusion), kind=kOutput, calls=%fused_computation.2 | convolution fusion | flops 816078848 | bytes 8519808 | tf_op jit(solution)/shard_map/dot_general | solution.py:40
  50.5 0.3 collective-permute-start.6
  50.8 1.6 collective-permute-start.4
  52.4 1.1 collective-permute-start.8
  53.5 265.9 %collective-permute-done.6 = bf16[256,8192]{1,0:T(8,128)(2,1)} collective-permute-done((bf16[256,8192]{1,0:T(8,128)(2,1)}, bf16[256,8192]{1,0:T(8,128)(2,1)}, u32[]{:S(2)}, u32[]{:S(2)}) %collective-permute-start.6) | collective-permute-done | bytes 4194336 | tf_op jit(solution)/shard_map/ppermute | solution.py:47
  319.4 0.0 all-gather.2.cloned.1.call-done
  319.4 0.0 copy-start.2
  319.4 10.0 %convolution_multiply_fusion.1 = f32[1024,256]{1,0:T(8,128)S(1)} fusion(bf16[1024,8192]{1,0:T(8,128)(2,1)} %all-gather.2.cloned.1.call-done, bf16[256,8192]{1,0:T(8,128)(2,1)} %collective-permute-done.6), kind=kOutput, calls=%fused_computation.17 | convolution fusion | flops 4295229440 | bytes 22020096 | tf_op jit(solution)/shard_map/dot_general | solution.py:54
  329.5 0.6 collective-permute-start.7
  330.1 81.0 %collective-permute-done.4 = bf16[256,8192]{1,0:T(8,128)(2,1)} collective-permute-done((bf16[256,8192]{1,0:T(8,128)(2,1)}, bf16[256,8192]{1,0:T(8,128)(2,1)}, u32[]{:S(2)}, u32[]{:S(2)}) %collective-permute-start.4) | collective-permute-done | bytes 4194336 | tf_op jit(solution)/shard_map/ppermute | solution.py:47
  411.1 0.0 copy-done.2
  411.1 6.7 %convolution_multiply_fusion.2 = f32[1024,256]{1,0:T(8,128)S(1)} fusion(bf16[1024,8192]{1,0:T(8,128)(2,1)S(1)} %copy-done.2, bf16[256,8192]{1,0:T(8,128)(2,1)} %collective-permute-done.4), kind=kOutput, calls=%fused_computation.18 | convolution fusion | flops 4295229440 | bytes 22020096 | tf_op jit(solution)/shard_map/dot_general | solution.py:54
  417.9 0.6 collective-permute-start.5
  418.5 9.3 %convolution_multiply_fusion.3 = f32[1024,256]{1,0:T(8,128)S(1)} fusion(bf16[1024,8192]{1,0:T(8,128)(2,1)} %all-gather.2.cloned.1.call-done, bf16[256,8192]{1,0:T(8,128)(2,1)} %fusion.1), kind=kOutput, calls=%fused_computation.19 | convolution fusion | flops 4295229440 | bytes 22020096 | tf_op jit(solution)/shard_map/dot_general | solution.py:54
  427.9 1.6 collective-permute-start.3
  429.5 0.0 collective-permute-done.8
  429.5 9.6 %convolution_multiply_fusion = f32[1024,256]{1,0:T(8,128)S(1)} fusion(bf16[1024,8192]{1,0:T(8,128)(2,1)} %all-gather.2.cloned.1.call-done, bf16[256,8192]{1,0:T(8,128)(2,1)} %collective-permute-done.8), kind=kOutput, calls=%fused_computation.16 | convolution fusion | flops 4295229440 | bytes 22020096 | tf_op jit(solution)/shard_map/dot_general | solution.py:54
  439.1 0.6 collective-permute-start.9
  439.7 0.0 collective-permute-done.5
  439.7 0.1 dynamic-slice_add_fusion.2
  439.8 4.2 collective-permute-done.3
  444.0 0.1 dynamic-slice_add_fusion.3
  444.1 1.1 broadcast_in_dim.10
  445.2 0.4 constant_dynamic-update-slice_fusion.3
  445.6 0.4 constant_dynamic-update-slice_fusion.2
  446.0 0.0 collective-permute-done.7
  446.0 0.1 dynamic-slice_add_fusion.1
  446.0 0.4 constant_dynamic-update-slice_fusion.1
  446.5 0.0 copy-start
  446.5 7.8 %collective-permute-done.9 = f32[1024,128]{1,0:T(8,128)S(1)} collective-permute-done((f32[1024,128]{1,0:T(8,128)S(1)}, f32[1024,128]{1,0:T(8,128)S(1)}, u32[]{:S(2)}, u32[]{:S(2)}) %collective-permute-start.9) | collective-permute-done | bytes 524320 | tf_op jit(solution)/shard_map/ppermute | solution.py:12
  454.3 0.1 dynamic-slice_add_fusion
  454.4 0.0 copy-done
  454.4 0.8 constant_dynamic-update-slice_fusion
  (5 shorter events, 0.2 us)
Async XLA Ops:
  6.5 17.6 %copy-start.1 = (s32[8192]{0:T(1024)S(1)}, s32[8192]{0:T(1024)}, u32[]{:S(2)}) copy-start(s32[8192]{0:T(1024)} %param.11) | copy-start | bytes 98308
  6.5 312.9 %all-gather.2.cloned.1.call-start = ((), (), s32[]{:S(2)}) async-start(), calls=%async_computation | async-start | bytes 20971520 | tf_op jit(solution)/shard_map/all_gather | solution.py:49
  6.5 17.6 %copy-start.3 = (bf16[256,8192]{1,0:T(8,128)(2,1)S(1)}, bf16[256,8192]{1,0:T(8,128)(2,1)}, u32[]{:S(2)}) copy-start(bf16[256,8192]{1,0:T(8,128)(2,1)} %param.7) | copy-start | bytes 12582916
  8.8 12.0 %collective-permute-start.1 = (f32[32]{0:T(128)S(1)}, f32[32]{0:T(128)S(1)}, u32[]{:S(2)}, u32[]{:S(2)}) collective-permute-start(f32[32]{0:T(128)S(1)} %select_reduce_fusion), channel_id=1, source_target_pairs={{0,1},{1,0},{2,3},{3,2},{4,5},{5,4},{6,7},{7,6},{8,9},{9,8},{10,11... | collective-permute-start | bytes 392 | tf_op jit(solution)/shard_map/ppermute | solution.py:12
  20.2 4.0 collective-permute-start
  30.9 13.1 %copy-start.4 = (bf16[256,8192]{1,0:T(8,128)(2,1)S(1)}, bf16[256,8192]{1,0:T(8,128)(2,1)}, u32[]{:S(2)}) copy-start(bf16[256,8192]{1,0:T(8,128)(2,1)} %param.8) | copy-start | bytes 12582916
  40.1 4.0 collective-permute-start.2
  50.5 269.0 %collective-permute-start.6 = (bf16[256,8192]{1,0:T(8,128)(2,1)}, bf16[256,8192]{1,0:T(8,128)(2,1)}, u32[]{:S(2)}, u32[]{:S(2)}) collective-permute-start(bf16[256,8192]{1,0:T(8,128)(2,1)} %fusion.1), channel_id=1, source_target_pairs={{0,16},{8,24},{16,0},{24,8},{1,17},{9,25},{17,1},{25,9},{2,18},{10... | collective-permute-start | bytes 12582920 | tf_op jit(solution)/shard_map/ppermute | solution.py:47
  50.8 360.3 %collective-permute-start.4 = (bf16[256,8192]{1,0:T(8,128)(2,1)}, bf16[256,8192]{1,0:T(8,128)(2,1)}, u32[]{:S(2)}, u32[]{:S(2)}) collective-permute-start(bf16[256,8192]{1,0:T(8,128)(2,1)} %fusion.1), channel_id=1, source_target_pairs={{0,8},{8,16},{16,24},{24,0},{1,9},{9,17},{17,25},{25,1},{2,10},{10... | collective-permute-start | bytes 12582920 | tf_op jit(solution)/shard_map/ppermute | solution.py:47
  52.4 377.1 %collective-permute-start.8 = (bf16[256,8192]{1,0:T(8,128)(2,1)}, bf16[256,8192]{1,0:T(8,128)(2,1)}, u32[]{:S(2)}, u32[]{:S(2)}) collective-permute-start(bf16[256,8192]{1,0:T(8,128)(2,1)} %fusion.1), channel_id=1, source_target_pairs={{0,24},{8,0},{16,8},{24,16},{1,25},{9,1},{17,9},{25,17},{2,26},{10... | collective-permute-start | bytes 12582920 | tf_op jit(solution)/shard_map/ppermute | solution.py:47
  319.4 91.7 %copy-start.2 = (bf16[1024,8192]{1,0:T(8,128)(2,1)S(1)}, bf16[1024,8192]{1,0:T(8,128)(2,1)}, u32[]{:S(2)}) copy-start(bf16[1024,8192]{1,0:T(8,128)(2,1)} %all-gather.2.cloned.1.call-done) | copy-start | bytes 50331652
  329.5 116.5 %collective-permute-start.7 = (f32[1024,128]{1,0:T(8,128)S(1)}, f32[1024,128]{1,0:T(8,128)S(1)}, u32[]{:S(2)}, u32[]{:S(2)}) collective-permute-start(f32[1024,128]{1,0:T(8,128)S(1)} %constant_dynamic-slice_fusion.1), channel_id=1, source_target_pairs={{0,1},{1,0},{2,3},{3,2},{4,5},{5,4},{6,7},{7,6},{8,9},{9,8},{10,11... | collective-permute-start | bytes 1572872 | tf_op jit(solution)/shard_map/ppermute | solution.py:12
  417.9 21.8 %collective-permute-start.5 = (f32[1024,128]{1,0:T(8,128)S(1)}, f32[1024,128]{1,0:T(8,128)S(1)}, u32[]{:S(2)}, u32[]{:S(2)}) collective-permute-start(f32[1024,128]{1,0:T(8,128)S(1)} %constant_dynamic-slice_fusion.2), channel_id=1, source_target_pairs={{0,1},{1,0},{2,3},{3,2},{4,5},{5,4},{6,7},{7,6},{8,9},{9,8},{10,11... | collective-permute-start | bytes 1572872 | tf_op jit(solution)/shard_map/ppermute | solution.py:12
  427.9 16.1 %collective-permute-start.3 = (f32[1024,128]{1,0:T(8,128)S(1)}, f32[1024,128]{1,0:T(8,128)S(1)}, u32[]{:S(2)}, u32[]{:S(2)}) collective-permute-start(f32[1024,128]{1,0:T(8,128)S(1)} %constant_dynamic-slice_fusion.3), channel_id=1, source_target_pairs={{0,1},{1,0},{2,3},{3,2},{4,5},{5,4},{6,7},{7,6},{8,9},{9,8},{10,11... | collective-permute-start | bytes 1572872 | tf_op jit(solution)/shard_map/ppermute | solution.py:12
  439.1 15.2 %collective-permute-start.9 = (f32[1024,128]{1,0:T(8,128)S(1)}, f32[1024,128]{1,0:T(8,128)S(1)}, u32[]{:S(2)}, u32[]{:S(2)}) collective-permute-start(f32[1024,128]{1,0:T(8,128)S(1)} %constant_dynamic-slice_fusion), channel_id=1, source_target_pairs={{0,1},{1,0},{2,3},{3,2},{4,5},{5,4},{6,7},{7,6},{8,9},{9,8},{10,11... | collective-permute-start | bytes 1572872 | tf_op jit(solution)/shard_map/ppermute | solution.py:12
  446.5 7.9 %copy-start = (f32[1024,4,1,128]{3,2,1,0:T(1,128)}, f32[1024,4,1,128]{3,2,1,0:T(1,128)S(1)}, u32[]{:S(2)}) copy-start(f32[1024,4,1,128]{3,2,1,0:T(1,128)S(1)} %constant_dynamic-update-slice_fusion.1) | copy-start | bytes 6291460
Sparse Core Ops, SparseCore 0:
  31.0 106.1 all-gather.1
